TPU v7x, 256 devices: a whole 4x4x8 slice. The times are simulated.
256 devices in a mesh: dp: 8 (over z), expert: 32 (over y, x, core).
Axes of the slice: x: 4, y: 4, z: 8, core: 2. Of those that a mesh axis runs over, the one named last changes fastest.
Arguments:
- tokens: bfloat16 [32, 16, 7168], P('expert', 'dp'), may hold values from -6 to 6
- tangent: bfloat16 [32, 16, 7168], P('expert', 'dp'), may hold values from -52 to 52
- route_ids: int32 [32, 16, 8], P('expert', 'dp'), may hold values from 0 to 31, all different within a row; in each aligned block of 16 rows (0 to 15, 16 to 31, ..., all dimensions but the last counted through in order) at most 8 rows name the same one
- gate_fixed: int32 [32, 16, 8], P('expert', 'dp'), may hold values from 4096 to 65535
- gate_proj: bfloat16 [32, 7168, 2048], P('expert', None, 'dp'), may hold values from -0.0625 to 0.0625
- up_proj: bfloat16 [32, 7168, 2048], P('expert', None, 'dp'), may hold values from -0.0625 to 0.0625
- down_proj: bfloat16 [32, 2048, 7168], P('expert', 'dp'), may hold values from -0.125 to 0.125
Outputs:
- next_tangent: bfloat16 [32, 16, 7168], P('expert', 'dp')
- lipschitz: float32 [], replicated
Inputs may be any that keep to these rules, and one draw needn't show every extreme that they name: `route_ids`: each token names 8 different experts; within one group of 16 tokens no expert is named by more than 8 tokens.
All inputs are finite; a program needn't handle non-finite values.
Results may differ from a plain program's by a relative error of at most 0.0065.
Values may be sent and summed in bfloat16 or wider, within the bound.
No kernel may reach another device: no remote copies, remote signals or barrier semaphores. Data moves between devices by JAX's collectives and lax.ppermute only.
A program may use at most 128 MiB of HBM per device.

v0:
```python
import jax
import jax.numpy as jnp
from jax import lax
from jax.sharding import PartitionSpec as P


def silu_parts(gate_pre):
    sigmoid_val = jax.nn.sigmoid(gate_pre)
    return (gate_pre * sigmoid_val, sigmoid_val * (1.0 + gate_pre * (1.0 - sigmoid_val)))


def contract_last(left, right):
    return lax.dot_general(
        left, right, (((1,), (1,)), ((), ())), preferred_element_type=jnp.float32
    )


def send_back(partial_value):
    return lax.all_to_all(partial_value, "expert", split_axis=0, concat_axis=0, tiled=True)


def body(tokens, tangent, route_ids, gate_fixed, gate_proj, up_proj, down_proj):
    model_width = tokens.shape[2]
    tok_dev = tokens.shape[1]
    experts = lax.axis_size("expert")
    col_tokens, col_tangent, col_ids, col_gates = (
        lax.all_gather(tokens[0], "dp", axis=0, tiled=True),
        lax.all_gather(tangent[0], "dp", axis=0, tiled=True),
        lax.all_gather(route_ids[0], "dp", axis=0, tiled=True),
        lax.all_gather(gate_fixed[0], "dp", axis=0, tiled=True),
    )
    col_count = col_tokens.shape[0]
    top_count = col_ids.shape[1]
    capacity = min(col_count, 2 * col_count * top_count // experts)
    slot_total = experts * capacity
    flat_ids = col_ids.reshape(-1)
    experts_all = jnp.arange(experts, dtype=jnp.int32)
    onehot = (flat_ids[:, None] == experts_all[None, :]).astype(jnp.int32)
    earlier = jnp.cumsum(onehot, axis=0) - onehot
    slot_place = jnp.sum(earlier * onehot, axis=1)
    target = flat_ids * capacity + slot_place
    places = jnp.arange(slot_total, dtype=jnp.int32)
    matches = target[:, None] == places[None, :]
    route_map = (
        jnp.sum(matches.reshape(col_count, top_count, slot_total), axis=1).astype(jnp.bfloat16).T
    )
    gate_vals = col_gates.reshape(-1).astype(jnp.float32) / 65536.0
    combine_map = jnp.sum(
        jnp.where(matches, gate_vals[:, None], 0.0).reshape(col_count, top_count, slot_total),
        axis=1,
    )
    send_in = (
        jnp.dot(route_map, col_tokens, preferred_element_type=jnp.float32)
        .astype(jnp.bfloat16)
        .reshape(experts, capacity, model_width)
    )
    send_dir = (
        jnp.dot(route_map, col_tangent, preferred_element_type=jnp.float32)
        .astype(jnp.bfloat16)
        .reshape(experts, capacity, model_width)
    )
    weight_gate = gate_proj[0]
    weight_up = up_proj[0]
    weight_down = down_proj[0]
    hidden_dev = weight_gate.shape[1]
    rows_in = lax.all_to_all(send_in, "expert", split_axis=0, concat_axis=0, tiled=True)
    rows_dir = lax.all_to_all(send_dir, "expert", split_axis=0, concat_axis=0, tiled=True)
    groups_here = rows_in.shape[0]
    slots_here = rows_in.shape[1]
    flat_in = rows_in.reshape(-1, model_width)
    flat_dir = rows_dir.reshape(-1, model_width)
    gate_pre = jnp.dot(flat_in, weight_gate, preferred_element_type=jnp.float32)
    up_pre = jnp.dot(flat_in, weight_up, preferred_element_type=jnp.float32)
    gate_dir = jnp.dot(flat_dir, weight_gate, preferred_element_type=jnp.float32)
    up_dir = jnp.dot(flat_dir, weight_up, preferred_element_type=jnp.float32)
    silu_value, silu_slope = silu_parts(gate_pre)
    jvp_hidden = (silu_slope * gate_dir * up_pre + silu_value * up_dir).astype(jnp.bfloat16)
    partial_value = jnp.dot(jvp_hidden, weight_down, preferred_element_type=jnp.float32)
    returned = send_back(partial_value.reshape(groups_here, slots_here, model_width))
    gate_coef = (silu_slope * up_pre).reshape(groups_here, slots_here, hidden_dev)
    up_coef = silu_value.reshape(groups_here, slots_here, hidden_dev)
    returned, gate_coef, up_coef = (returned, gate_coef, up_coef)
    product_part = jnp.dot(
        combine_map,
        returned.reshape(slot_total, -1),
        precision=lax.Precision.HIGHEST,
        preferred_element_type=jnp.float32,
    )
    product_bf = lax.psum(product_part, "dp").astype(jnp.bfloat16)
    send_prod = (
        jnp.dot(route_map, product_bf, preferred_element_type=jnp.float32)
        .astype(jnp.bfloat16)
        .reshape(experts, capacity, model_width)
    )
    received = lax.all_to_all(send_prod, "expert", split_axis=0, concat_axis=0, tiled=True)
    grad_hidden = contract_last(received.reshape(slot_total, model_width), weight_down)
    grad_gate = (grad_hidden * gate_coef.reshape(slot_total, hidden_dev)).astype(jnp.bfloat16)
    grad_up = (grad_hidden * up_coef.reshape(slot_total, hidden_dev)).astype(jnp.bfloat16)
    vjp_part = contract_last(grad_gate, weight_gate) + contract_last(grad_up, weight_up)
    returned_two = send_back(vjp_part.reshape(experts, capacity, model_width))
    result_part = jnp.dot(
        combine_map,
        returned_two.reshape(slot_total, -1),
        precision=lax.Precision.HIGHEST,
        preferred_element_type=jnp.float32,
    )
    result = lax.psum_scatter(result_part, "dp", scatter_dimension=0, tiled=True)
    probe_f = tangent[0].astype(jnp.float32)
    probe_result, result_sq, probe_sq = lax.psum(
        (jnp.sum(probe_f * result), jnp.sum(result * result), jnp.sum(probe_f * probe_f)),
        ("dp", "expert"),
    )
    total_cells = lax.axis_size("dp") * lax.axis_size("expert") * tok_dev * model_width
    next_tangent = (result * lax.rsqrt(result_sq / total_cells + 1e-06)).astype(jnp.bfloat16)
    lipschitz = jnp.sqrt(probe_result / probe_sq)
    return (next_tangent[None], lipschitz)


def solution(mesh):
    return jax.shard_map(
        body,
        mesh=mesh,
        in_specs=(
            P("expert", "dp", None),
            P("expert", "dp", None),
            P("expert", "dp", None),
            P("expert", "dp", None),
            P("expert", None, "dp"),
            P("expert", None, "dp"),
            P("expert", "dp", None),
        ),
        out_specs=(P("expert", "dp", None), P()),
        check_vma=False,
    )
```

profile of v0, /device:TPU:1, one launch (start us, length us, event | category | flops | bytes accessed | tf_op | source)
XLA Modules:
  0.0 622.9 jit_solution(1392663835908994589)
XLA Ops:
  7.2 16.7 %all-gather = s32[1,16,8]{2,0,1:T(1,128)S(1)} all-gather(s32[1,2,8]{2,0,1:T(1,128)} %bitcast.102), channel_id=2, replica_groups=mesh['dp'=8,'expert'=32] {'dp'}, dimensions={1}, use_global_device_ids=true | all-gather | bytes 576 | tf_op jit(solution)/shard_map/all_gather | solution.py:29
  23.9 0.1 copy.40
  23.9 0.5 broadcast.53
  24.4 0.7 reduce.3
  25.1 0.1 eq.30
  25.2 0.1 fusion.68
  25.3 0.2 reduce_window_sum.11
  25.5 0.2 select_reduce_fusion.1
  25.7 0.1 reduce_sum.57
  25.7 0.1 copy.41
  25.8 0.1 copy.42
  25.9 0.1 convert_reduce_fusion
  26.0 0.8 copy.46
  26.8 19.3 %all-gather.2 = bf16[1,16,7168]{2,0,1:T(2,128)(2,1)S(1)} all-gather(bf16[1,2,7168]{2,0,1:T(2,128)(2,1)S(1)} %copy.46), channel_id=4, replica_groups=mesh['dp'=8,'expert'=32] {'dp'}, dimensions={1}, use_global_device_ids=true | all-gather | bytes 258048 | tf_op jit(solution)/shard_map/all_gather | solution.py:27
  46.1 3.0 fusion.1
  49.1 17.6 %all-to-all-start = ((bf16[32,8,7168]{2,1,0:T(8,128)(2,1)}), bf16[32,8,7168]{2,1,0:T(8,128)(2,1)}, u32[]{:S(2)}, u32[]{:S(2)}) async-start(bf16[32,8,7168]{2,1,0:T(8,128)(2,1)} %fusion.1), calls=%async_computation | async-start | bytes 7340032 | tf_op jit(solution)/shard_map/all_to_all | solution.py:66
  66.9 21.6 %all-gather.3 = bf16[1,16,7168]{2,0,1:T(2,128)(2,1)S(1)} all-gather(bf16[1,2,7168]{2,0,1:T(2,128)(2,1)S(1)} %copy.47), channel_id=5, replica_groups=mesh['dp'=8,'expert'=32] {'dp'}, dimensions={1}, use_global_device_ids=true | all-gather | bytes 258048 | tf_op jit(solution)/shard_map/all_gather | solution.py:28
  88.4 3.0 fusion.2
  91.4 20.8 %all-to-all-done = bf16[32,8,7168]{2,1,0:T(8,128)(2,1)} async-done(((bf16[32,8,7168]{2,1,0:T(8,128)(2,1)}), bf16[32,8,7168]{2,1,0:T(8,128)(2,1)}, u32[]{:S(2)}, u32[]{:S(2)}) %all-to-all-start) | async-done | bytes 3670048 | tf_op jit(solution)/shard_map/all_to_all | solution.py:66
  112.2 7.2 %all-to-all-start.1 = ((bf16[32,8,7168]{2,1,0:T(8,128)(2,1)}), bf16[32,8,7168]{2,1,0:T(8,128)(2,1)}, u32[]{:S(2)}, u32[]{:S(2)}) async-start(bf16[32,8,7168]{2,1,0:T(8,128)(2,1)} %fusion.2), calls=%async_computation.1 | async-start | bytes 7340032 | tf_op jit(solution)/shard_map/all_to_all | solution.py:67
  119.5 4.4 fusion.24
  123.9 3.2 fusion.16
  127.1 37.5 %all-to-all-done.1 = bf16[32,8,7168]{2,1,0:T(8,128)(2,1)} async-done(((bf16[32,8,7168]{2,1,0:T(8,128)(2,1)}), bf16[32,8,7168]{2,1,0:T(8,128)(2,1)}, u32[]{:S(2)}, u32[]{:S(2)}) %all-to-all-start.1) | async-done | bytes 3670048 | tf_op jit(solution)/shard_map/all_to_all | solution.py:67
  164.6 4.3 fusion.43
  168.9 11.2 %fusion.10 = f32[32,8,7168]{2,1,0:T(8,128)} fusion(bf16[1,256,7168]{2,1,0:T(8,128)(2,1)} %param.13, f32[256,256]{1,0:T(8,128)S(1)} %fusion.43, f32[256,256]{1,0:T(8,128)S(1)} %fusion.16, bf16[1,7168,256]{2,1,0:T(8,128)(2,1)} %param.11, bf16[32,8,7168]{2,1,0:T(8,128)(2,1)} %all-to-all-done.1, f32[256,256]{1,0:T(8,128)S(1)} %fusion.24), kind=kOutput, calls=%fused_computation.14 | convolution fusion | flops 1879769088 | bytes 19136512 | tf_op jit(solution)/shard_map/dot_general | solution.py:78
  180.0 7.8 %all-to-all-start.2 = ((f32[32,8,7168]{2,1,0:T(8,128)}), f32[32,8,7168]{2,1,0:T(8,128)}, u32[]{:S(2)}, u32[]{:S(2)}) async-start(f32[32,8,7168]{2,1,0:T(8,128)} %fusion.10), calls=%async_computation.2 | async-start | bytes 14680064 | tf_op jit(solution)/shard_map/all_to_all | solution.py:19
  187.8 0.0 all-reduce.5.cloned.1.call-start
  187.9 11.6 %all-gather.1 = s32[1,16,8]{2,0,1:T(1,128)S(1)} all-gather(s32[1,2,8]{2,0,1:T(1,128)S(1)} %bitcast.103), channel_id=3, replica_groups=mesh['dp'=8,'expert'=32] {'dp'}, dimensions={1}, use_global_device_ids=true | all-gather | bytes 576 | tf_op jit(solution)/shard_map/all_gather | solution.py:30
  199.5 0.1 copy.44
  199.6 0.1 copy.45
  199.7 0.1 select_reduce_fusion
  199.8 75.2 %all-to-all-done.2 = f32[32,8,7168]{2,1,0:T(8,128)} async-done(((f32[32,8,7168]{2,1,0:T(8,128)}), f32[32,8,7168]{2,1,0:T(8,128)}, u32[]{:S(2)}, u32[]{:S(2)}) %all-to-all-start.2) | async-done | bytes 7340064 | tf_op jit(solution)/shard_map/all_to_all | solution.py:19
  275.0 5.7 fusion.6
  280.7 26.0 %all-reduce.6 = bf16[16,7168]{1,0:T(8,128)(2,1)S(1)} all-reduce(f32[16,7168]{1,0:T(8,128)S(1)} %fusion.6), channel_id=1, replica_groups=mesh['dp'=8,'expert'=32] {'dp'}, use_global_device_ids=true, to_apply=%region_4.5 | all-reduce | flops 114688 | bytes 688128 | tf_op jit(solution)/shard_map/psum | solution.py:89
  306.7 1.1 fusion.3
  307.8 60.0 %all_to_all.25 = bf16[32,8,7168]{2,1,0:T(8,128)(2,1)S(1)} all-to-all(bf16[32,8,7168]{2,1,0:T(8,128)(2,1)S(1)} %fusion.3), channel_id=1, replica_groups=mesh['dp'=8,'expert'=32] {'expert'}, dimensions={0} | all-to-all | bytes 7340032 | tf_op jit(solution)/shard_map/all_to_all | solution.py:95
  367.9 1.1 fusion.8
  369.0 0.9 copy-done
  369.9 1.2 fusion.21
  371.1 0.9 copy-done.3
  371.9 1.2 fusion
  373.1 88.2 %all_to_all.26 = f32[32,8,7168]{2,1,0:T(8,128)S(1)} all-to-all(f32[32,8,7168]{2,1,0:T(8,128)S(1)} %fusion), channel_id=1, replica_groups=mesh['dp'=8,'expert'=32] {'expert'}, dimensions={0} | all-to-all | bytes 14680064 | tf_op jit(solution)/shard_map/all_to_all | solution.py:19
  461.4 4.3 fusion.4
  465.7 0.6 dynamic-slice
  467.0 62.5 %all-reduce.5.cloned.1.call-done = f32[16,7168]{1,0:T(8,128)} async-done(((f32[16,7168]{1,0:T(8,128)}), f32[16,7168]{1,0:T(8,128)}) %all-reduce.5.cloned.1.call-update) | async-done | bytes 458768
  529.5 1.7 fusion.69
  531.2 80.1 %all-reduce.1 = (f32[]{:T(128)}, f32[]{:T(128)}, f32[]{:T(128)}) all-reduce(f32[]{:T(128)} %get-tuple-element.3, f32[]{:T(128)} %get-tuple-element.2, f32[]{:T(128)} %get-tuple-element.4), channel_id=1, replica_groups=mesh['dp'=8,'expert'=32] {'dp','expert'}, use_global_device_ids=true, to_apply=%region_7.8 | all-reduce | flops 3 | bytes 24 | tf_op jit(solution)/shard_map/psum | solution.py:109
  613.3 1.6 fusion.72
  (16 shorter events, 0.1 us)
Async XLA Ops:
  49.1 17.7 %copy-start.4 = (bf16[1,2,7168]{2,1,0:T(2,128)(2,1)S(1)}, bf16[1,2,7168]{2,1,0:T(2,128)(2,1)}, u32[]{:S(2)}) copy-start(bf16[1,2,7168]{2,1,0:T(2,128)(2,1)} %param.8) | copy-start | bytes 86020
  49.1 63.1 %all-to-all-start = ((bf16[32,8,7168]{2,1,0:T(8,128)(2,1)}), bf16[32,8,7168]{2,1,0:T(8,128)(2,1)}, u32[]{:S(2)}, u32[]{:S(2)}) async-start(bf16[32,8,7168]{2,1,0:T(8,128)(2,1)} %fusion.1), calls=%async_computation | async-start | bytes 7340032 | tf_op jit(solution)/shard_map/all_to_all | solution.py:66
  112.2 52.4 %all-to-all-start.1 = ((bf16[32,8,7168]{2,1,0:T(8,128)(2,1)}), bf16[32,8,7168]{2,1,0:T(8,128)(2,1)}, u32[]{:S(2)}, u32[]{:S(2)}) async-start(bf16[32,8,7168]{2,1,0:T(8,128)(2,1)} %fusion.2), calls=%async_computation.1 | async-start | bytes 7340032 | tf_op jit(solution)/shard_map/all_to_all | solution.py:67
  119.4 4.4 copy-start.2
  180.0 7.9 %copy-start.5 = (s32[1,2,8]{2,1,0:T(2,128)S(1)}, s32[1,2,8]{2,1,0:T(2,128)}, u32[]{:S(2)}) copy-start(s32[1,2,8]{2,1,0:T(2,128)} %param.10) | copy-start | bytes 196
  180.0 95.0 %all-to-all-start.2 = ((f32[32,8,7168]{2,1,0:T(8,128)}), f32[32,8,7168]{2,1,0:T(8,128)}, u32[]{:S(2)}, u32[]{:S(2)}) async-start(f32[32,8,7168]{2,1,0:T(8,128)} %fusion.10), calls=%async_computation.2 | async-start | bytes 14680064 | tf_op jit(solution)/shard_map/all_to_all | solution.py:19
  187.8 341.6 %all-reduce.5.cloned.1.call-start = ((), (), s32[]{:S(2)}) async-start(), calls=%async_computation.5 | async-start | bytes 917504
  307.8 60.0 %copy-start.1 = (bf16[1,256,7168]{2,1,0:T(8,128)(2,1)S(1)}, bf16[1,256,7168]{2,1,0:T(8,128)(2,1)}, u32[]{:S(2)}) copy-start(bf16[1,256,7168]{2,1,0:T(8,128)(2,1)} %param.13) | copy-start | bytes 11010052
  367.9 2.0 copy-start
  369.9 2.0 copy-start.3
  461.4 4.4 copy-start.6
Sparse Core Ops, SparseCore 0:
  465.8 63.5 all-reduce.4
where the time goes:
time: 624 us; the launch traced here: 623 us
  blocking collectives  323 us (52%)
  waiting for transfers between devices  196 us (31%)
  matrix products  43.7 us (7%)
  starting transfers between devices  32.7 us (5%)
  between operations  18.1 us (3%)
    all_to_all x1, blocking collectives, send_back(): lax.all_to_all(partial_value, 'expert', split_axis=0, concat_axis=0, tile...  88.2 us
    psum x1, blocking collectives, body(): lax.psum((jnp.sum(probe_f * result), jnp.sum(result * result), jnp.sum(pr...  80.1 us
    all_to_all x1, waiting for transfers between devices, send_back(): lax.all_to_all(partial_value, 'expert', split_axis=0, concat_axis=0, tile...  75.2 us
    unnamed x2, waiting for transfers between devices  62.5 us
    all_to_all x1, blocking collectives, body(): lax.all_to_all(send_prod, 'expert', split_axis=0, concat_axis=0, tiled=True)  60 us
    all_to_all x1, waiting for transfers between devices, body(): lax.all_to_all(send_dir, 'expert', split_axis=0, concat_axis=0, tiled=True)  37.5 us
    psum x1, blocking collectives, body(): product_bf = lax.psum(product_part, 'dp').astype(jnp.bfloat16)  26 us
    all_gather x1, blocking collectives, body(): lax.all_gather(tangent[0], 'dp', axis=0, tiled=True)  21.6 us
  transfers between devices with their start and end apart: 4, of which 4 were waited for; matrix products, arithmetic and copies ran while one was open for 2% of the time, Pallas kernels for 0%

commit v1 on v0

--- a/solution.py
+++ b/solution.py
@@ -86,7 +86,12 @@
         precision=lax.Precision.HIGHEST,
         preferred_element_type=jnp.float32,
     )
-    product_bf = lax.psum(product_part, "dp").astype(jnp.bfloat16)
+
+    def proceed_orders(row_data, mesh_name):
+        r_now = lax.all_gather(row_data, mesh_name).sum(axis=0)
+        return r_now
+
+    product_bf = proceed_orders(product_part, "dp").astype(jnp.bfloat16)
     send_prod = (
         jnp.dot(route_map, product_bf, preferred_element_type=jnp.float32)
         .astype(jnp.bfloat16)

time: 624 us -> 643 us (1.030)
  waiting for transfers between devices: 196 us -> 244 us
  blocking collectives: 323 us -> 290 us
    all_gather x0 -> x1, waiting for transfers between devices: none -> 47.8 us  [proceed_orders(): r_now = lax.all_gather(row_data, mesh_name).sum(axis=0)]
    psum x1 -> x0, blocking collectives: 26 us -> none  [body(): product_bf = lax.psum(product_part, 'dp').astype(jnp.bfloat16)]
    all_to_all x1, blocking collectives: 60 us -> 52.9 us  [body(): lax.all_to_all(send_prod, 'expert', split_axis=0, concat_axis=0, tiled=True)]
    unnamed x2 -> x3, waiting for transfers between devices: 62.5 us -> 63.3 us
  transfers between devices with their start and end apart: 4 -> 5, of which waited for: 4 -> 5; matrix products, arithmetic and copies ran while one was open for 2% -> 2% of each run, Pallas kernels for 0% -> 0%
where the time goes in v1:
time: 643 us; the launch traced here: 642 us
  blocking collectives  290 us (45%)
  waiting for transfers between devices  244 us (38%)
  matrix products  45.4 us (7%)
  starting transfers between devices  32.7 us (5%)
  between operations  18.1 us (3%)
  other arithmetic  6.88 us (1%)
    all_to_all x1, blocking collectives, send_back(): lax.all_to_all(partial_value, 'expert', split_axis=0, concat_axis=0, tile...  88.1 us
    psum x1, blocking collectives, body(): lax.psum((jnp.sum(probe_f * result), jnp.sum(result * result), jnp.sum(pr...  80.1 us
    all_to_all x1, waiting for transfers between devices, send_back(): lax.all_to_all(partial_value, 'expert', split_axis=0, concat_axis=0, tile...  75.2 us
    unnamed x3, waiting for transfers between devices  63.3 us
    all_to_all x1, blocking collectives, body(): lax.all_to_all(send_prod, 'expert', split_axis=0, concat_axis=0, tiled=True)  52.9 us
    all_gather x1, waiting for transfers between devices, proceed_orders(): r_now = lax.all_gather(row_data, mesh_name).sum(axis=0)  47.8 us
    all_to_all x1, waiting for transfers between devices, body(): lax.all_to_all(send_dir, 'expert', split_axis=0, concat_axis=0, tiled=True)  37.5 us
    all_gather x1, blocking collectives, body(): lax.all_gather(tangent[0], 'dp', axis=0, tiled=True)  21.6 us
  transfers between devices with their start and end apart: 5, of which 5 were waited for; matrix products, arithmetic and copies ran while one was open for 2% of the time, Pallas kernels for 0%

profile of v1, /device:TPU:1, one launch (start us, length us, event | category | flops | bytes accessed | tf_op | source)
XLA Modules:
  0.0 642.1 jit_solution(5502922496966831543)
XLA Ops:
  7.2 16.7 %all-gather = s32[1,16,8]{2,0,1:T(1,128)S(1)} all-gather(s32[1,2,8]{2,0,1:T(1,128)} %bitcast.104), channel_id=2, replica_groups=mesh['dp'=8,'expert'=32] {'dp'}, dimensions={1}, use_global_device_ids=true | all-gather | bytes 576 | tf_op jit(solution)/shard_map/all_gather | solution.py:29
  23.9 0.1 copy.40
  23.9 0.5 broadcast.53
  24.4 0.7 reduce.3
  25.1 0.1 eq.30
  25.2 0.1 fusion.68
  25.3 0.2 reduce_window_sum.11
  25.5 0.2 select_reduce_fusion.1
  25.7 0.1 reduce_sum.66
  25.7 0.1 copy.41
  25.8 0.1 copy.42
  25.9 0.1 convert_reduce_fusion
  26.0 0.8 copy.46
  26.8 19.3 %all-gather.2 = bf16[1,16,7168]{2,0,1:T(2,128)(2,1)S(1)} all-gather(bf16[1,2,7168]{2,0,1:T(2,128)(2,1)S(1)} %copy.46), channel_id=4, replica_groups=mesh['dp'=8,'expert'=32] {'dp'}, dimensions={1}, use_global_device_ids=true | all-gather | bytes 258048 | tf_op jit(solution)/shard_map/all_gather | solution.py:27
  46.1 3.0 fusion.1
  49.1 17.6 %all-to-all-start = ((bf16[32,8,7168]{2,1,0:T(8,128)(2,1)}), bf16[32,8,7168]{2,1,0:T(8,128)(2,1)}, u32[]{:S(2)}, u32[]{:S(2)}) async-start(bf16[32,8,7168]{2,1,0:T(8,128)(2,1)} %fusion.1), calls=%async_computation | async-start | bytes 7340032 | tf_op jit(solution)/shard_map/all_to_all | solution.py:66
  66.8 21.6 %all-gather.3 = bf16[1,16,7168]{2,0,1:T(2,128)(2,1)S(1)} all-gather(bf16[1,2,7168]{2,0,1:T(2,128)(2,1)S(1)} %copy.47), channel_id=5, replica_groups=mesh['dp'=8,'expert'=32] {'dp'}, dimensions={1}, use_global_device_ids=true | all-gather | bytes 258048 | tf_op jit(solution)/shard_map/all_gather | solution.py:28
  88.4 3.0 fusion.2
  91.4 20.7 %all-to-all-done = bf16[32,8,7168]{2,1,0:T(8,128)(2,1)} async-done(((bf16[32,8,7168]{2,1,0:T(8,128)(2,1)}), bf16[32,8,7168]{2,1,0:T(8,128)(2,1)}, u32[]{:S(2)}, u32[]{:S(2)}) %all-to-all-start) | async-done | bytes 3670048 | tf_op jit(solution)/shard_map/all_to_all | solution.py:66
  112.1 7.2 %all-to-all-start.1 = ((bf16[32,8,7168]{2,1,0:T(8,128)(2,1)}), bf16[32,8,7168]{2,1,0:T(8,128)(2,1)}, u32[]{:S(2)}, u32[]{:S(2)}) async-start(bf16[32,8,7168]{2,1,0:T(8,128)(2,1)} %fusion.2), calls=%async_computation.1 | async-start | bytes 7340032 | tf_op jit(solution)/shard_map/all_to_all | solution.py:67
  119.4 4.4 fusion.24
  123.8 3.2 fusion.16
  127.0 37.5 %all-to-all-done.1 = bf16[32,8,7168]{2,1,0:T(8,128)(2,1)} async-done(((bf16[32,8,7168]{2,1,0:T(8,128)(2,1)}), bf16[32,8,7168]{2,1,0:T(8,128)(2,1)}, u32[]{:S(2)}, u32[]{:S(2)}) %all-to-all-start.1) | async-done | bytes 3670048 | tf_op jit(solution)/shard_map/all_to_all | solution.py:67
  164.5 4.3 fusion.43
  168.8 11.2 %fusion.10 = f32[32,8,7168]{2,1,0:T(8,128)} fusion(bf16[1,256,7168]{2,1,0:T(8,128)(2,1)} %param.13, f32[256,256]{1,0:T(8,128)S(1)} %fusion.43, f32[256,256]{1,0:T(8,128)S(1)} %fusion.16, bf16[1,7168,256]{2,1,0:T(8,128)(2,1)} %param.11, bf16[32,8,7168]{2,1,0:T(8,128)(2,1)} %all-to-all-done.1, f32[256,256]{1,0:T(8,128)S(1)} %fusion.24), kind=kOutput, calls=%fused_computation.14 | convolution fusion | flops 1879769088 | bytes 19136512 | tf_op jit(solution)/shard_map/dot_general | solution.py:78
  180.0 7.8 %all-to-all-start.2 = ((f32[32,8,7168]{2,1,0:T(8,128)}), f32[32,8,7168]{2,1,0:T(8,128)}, u32[]{:S(2)}, u32[]{:S(2)}) async-start(f32[32,8,7168]{2,1,0:T(8,128)} %fusion.10), calls=%async_computation.2 | async-start | bytes 14680064 | tf_op jit(solution)/shard_map/all_to_all | solution.py:19
  187.9 11.6 %all-gather.1 = s32[1,16,8]{2,0,1:T(1,128)S(1)} all-gather(s32[1,2,8]{2,0,1:T(1,128)S(1)} %bitcast.105), channel_id=3, replica_groups=mesh['dp'=8,'expert'=32] {'dp'}, dimensions={1}, use_global_device_ids=true | all-gather | bytes 576 | tf_op jit(solution)/shard_map/all_gather | solution.py:30
  199.5 0.1 copy.44
  199.6 0.1 copy.45
  199.6 0.1 select_reduce_fusion
  199.8 75.2 %all-to-all-done.2 = f32[32,8,7168]{2,1,0:T(8,128)} async-done(((f32[32,8,7168]{2,1,0:T(8,128)}), f32[32,8,7168]{2,1,0:T(8,128)}, u32[]{:S(2)}, u32[]{:S(2)}) %all-to-all-start.2) | async-done | bytes 7340064 | tf_op jit(solution)/shard_map/all_to_all | solution.py:19
  275.0 7.4 %fusion.6 = f32[16,7168]{1,0:T(8,128)} fusion(f32[16,256]{1,0:T(8,128)S(1)} %select_reduce_fusion, f32[32,8,7168]{2,1,0:T(8,128)} %all-to-all-done.2), kind=kOutput, calls=%fused_computation.10 | convolution fusion | flops 352321536 | bytes 7815168 | tf_op jit(solution)/shard_map/dot_general | solution.py:83
  282.4 47.8 %all-gather.7.cloned.1.call-done = f32[128,7168]{1,0:T(8,128)} async-done(((f32[16,7168]{1,0:T(8,128)}), f32[128,7168]{1,0:T(8,128)}) %all-gather.7.cloned.1.call-update) | async-done | bytes 3670032 | tf_op jit(solution)/shard_map/all_gather | solution.py:91
  330.2 2.2 reduce_sum.69
  332.4 1.1 fusion.3
  333.6 52.9 %all_to_all.25 = bf16[32,8,7168]{2,1,0:T(8,128)(2,1)S(1)} all-to-all(bf16[32,8,7168]{2,1,0:T(8,128)(2,1)S(1)} %fusion.3), channel_id=1, replica_groups=mesh['dp'=8,'expert'=32] {'expert'}, dimensions={0} | all-to-all | bytes 7340032 | tf_op jit(solution)/shard_map/all_to_all | solution.py:100
  386.5 1.1 fusion.8
  387.6 0.9 copy-done
  388.5 1.2 fusion.21
  389.7 0.9 copy-done.3
  390.5 1.2 fusion
  391.7 88.1 %all_to_all.26 = f32[32,8,7168]{2,1,0:T(8,128)S(1)} all-to-all(f32[32,8,7168]{2,1,0:T(8,128)S(1)} %fusion), channel_id=1, replica_groups=mesh['dp'=8,'expert'=32] {'expert'}, dimensions={0} | all-to-all | bytes 14680064 | tf_op jit(solution)/shard_map/all_to_all | solution.py:19
  479.8 4.3 fusion.4
  484.2 0.6 dynamic-slice
  485.4 63.2 %all-reduce.4.cloned.1.call-done = f32[16,7168]{1,0:T(8,128)} async-done(((f32[16,7168]{1,0:T(8,128)}), f32[16,7168]{1,0:T(8,128)}) %all-reduce.4.cloned.1.call-update) | async-done | bytes 458768
  548.6 1.7 fusion.69
  550.3 80.1 %all-reduce.1 = (f32[]{:T(128)}, f32[]{:T(128)}, f32[]{:T(128)}) all-reduce(f32[]{:T(128)} %get-tuple-element.3, f32[]{:T(128)} %get-tuple-element.2, f32[]{:T(128)} %get-tuple-element.4), channel_id=1, replica_groups=mesh['dp'=8,'expert'=32] {'dp','expert'}, use_global_device_ids=true, to_apply=%region_7.8 | all-reduce | flops 3 | bytes 24 | tf_op jit(solution)/shard_map/psum | solution.py:114
  632.5 1.6 fusion.72
  (19 shorter events, 0.2 us)
Async XLA Ops:
  49.1 17.7 %copy-start.4 = (bf16[1,2,7168]{2,1,0:T(2,128)(2,1)S(1)}, bf16[1,2,7168]{2,1,0:T(2,128)(2,1)}, u32[]{:S(2)}) copy-start(bf16[1,2,7168]{2,1,0:T(2,128)(2,1)} %param.8) | copy-start | bytes 86020
  49.1 63.1 %all-to-all-start = ((bf16[32,8,7168]{2,1,0:T(8,128)(2,1)}), bf16[32,8,7168]{2,1,0:T(8,128)(2,1)}, u32[]{:S(2)}, u32[]{:S(2)}) async-start(bf16[32,8,7168]{2,1,0:T(8,128)(2,1)} %fusion.1), calls=%async_computation | async-start | bytes 7340032 | tf_op jit(solution)/shard_map/all_to_all | solution.py:66
  112.1 52.4 %all-to-all-start.1 = ((bf16[32,8,7168]{2,1,0:T(8,128)(2,1)}), bf16[32,8,7168]{2,1,0:T(8,128)(2,1)}, u32[]{:S(2)}, u32[]{:S(2)}) async-start(bf16[32,8,7168]{2,1,0:T(8,128)(2,1)} %fusion.2), calls=%async_computation.1 | async-start | bytes 7340032 | tf_op jit(solution)/shard_map/all_to_all | solution.py:67
  119.4 4.4 copy-start.2
  180.0 7.9 %copy-start.5 = (s32[1,2,8]{2,1,0:T(2,128)S(1)}, s32[1,2,8]{2,1,0:T(2,128)}, u32[]{:S(2)}) copy-start(s32[1,2,8]{2,1,0:T(2,128)} %param.10) | copy-start | bytes 196
  180.0 95.0 %all-to-all-start.2 = ((f32[32,8,7168]{2,1,0:T(8,128)}), f32[32,8,7168]{2,1,0:T(8,128)}, u32[]{:S(2)}, u32[]{:S(2)}) async-start(f32[32,8,7168]{2,1,0:T(8,128)} %fusion.10), calls=%async_computation.2 | async-start | bytes 14680064 | tf_op jit(solution)/shard_map/all_to_all | solution.py:19
  187.8 142.4 %all-gather.7.cloned.1.call-start = ((), (), s32[]{:S(2)}) async-start(), calls=%async_computation.5 | async-start | bytes 4128768 | tf_op jit(solution)/shard_map/all_gather | solution.py:91
  282.4 266.2 %all-reduce.4.cloned.1.call-start = ((), (), s32[]{:S(2)}) async-start(), calls=%async_computation.6 | async-start | bytes 917504
  333.6 52.9 %copy-start.1 = (bf16[1,256,7168]{2,1,0:T(8,128)(2,1)S(1)}, bf16[1,256,7168]{2,1,0:T(8,128)(2,1)}, u32[]{:S(2)}) copy-start(bf16[1,256,7168]{2,1,0:T(8,128)(2,1)} %param.13) | copy-start | bytes 11010052
  386.5 2.0 copy-start
  388.5 2.0 copy-start.3
  479.8 4.4 copy-start.6
Sparse Core Ops, SparseCore 0:
  282.5 47.6 all-gather.6
  484.3 64.3 all-reduce.3
